TPU v7x, 32 devices: a whole 2x2x4 slice. The times are simulated.
32 devices in a mesh: row: 8 (over z, y), col: 4 (over x, core).
Axes of the slice: x: 2, y: 2, z: 4, core: 2. Of those that a mesh axis runs over, the one named last changes fastest.
Arguments:
- x_t: bfloat16 [128, 8192], P('col', 'row'), may hold values from -6 to 6
- tiles: bfloat16 [64, 128, 128], P('row'), may hold values from -0.375 to 0.375
- tile_owner: int32 [64, 1], P('row'), may hold values from 0 to 7; in each aligned block of 8 rows (0 to 7, 8 to 15, ...) at most 2 rows name the same one
- tile_local: int32 [64, 2], P('row'), may hold values from 0 to 7
- weight: bfloat16 [128, 256], replicated, may hold values from -0.5 to 0.5
- cotangent: bfloat16 [8192, 256], P('row'), may hold values from -0.0625 to 0.0625
Outputs:
- act: bfloat16 [8192, 256], P('row')
- grad_w: float32 [128, 256], P('col')
Inputs may be any that keep to these rules, and one draw needn't show every extreme that they name: `tile_owner`: within the 8 stored tiles of one index of row (aligned blocks of 8 rows) no owner appears more than 2 times, and some owner appears exactly 2 times.
All inputs are finite; a program needn't handle non-finite values.
Results may differ from a plain program's by a relative error of at most 0.0059.
Values may be sent and summed in bfloat16 or wider, within the bound.
No kernel may reach another device: no remote copies, remote signals or barrier semaphores. Data moves between devices by JAX's collectives and lax.ppermute only.
A program may use at most 64 MiB of HBM per device.

v0:
```python
import jax
import jax.numpy as jnp
from jax import lax
from jax.sharding import PartitionSpec as P


def gather_groups(z_part, n_col):
    if n_col == 1:
        return z_part
    me = lax.axis_index("col")
    parts = [z_part]
    for k in range(1, n_col):
        perm = [(i, (i + k) % n_col) for i in range(n_col)]
        parts.append(lax.ppermute(z_part, "col", perm))
    stacked = jnp.stack(parts)
    order = (me - jnp.arange(n_col, dtype=jnp.int32)) % n_col
    full = jnp.take(stacked, order, axis=0)
    return full.reshape(n_col * z_part.shape[0], z_part.shape[1])


def sum_over_row(x, n_row):
    if n_row & n_row - 1:
        return lax.psum(x, "row")
    k = 1
    while k < n_row:
        perm = [(i, i ^ k) for i in range(n_row)]
        x = x + lax.ppermute(x, "row", perm)
        k *= 2
    return x


def body(x_t, tiles, tile_owner, tile_local, weight, cotangent):
    n_row = lax.axis_size("row")
    n_col = lax.axis_size("col")
    n_tiles, tile_dim = (tiles.shape[0], tiles.shape[1])
    feat_q, rows = x_t.shape
    n_blocks = rows // tile_dim
    capacity = 2 * (n_tiles // n_row)
    xb = x_t.reshape(feat_q, n_blocks, tile_dim).transpose(1, 0, 2)
    flat_blocks = xb.reshape(n_blocks, feat_q * tile_dim)
    owner = tile_owner[:, 0]
    row_local = tile_local[:, 0]
    col_local = tile_local[:, 1]
    owner_hot = (owner[:, None] == jnp.arange(n_row, dtype=jnp.int32)[None, :]).astype(jnp.int32)
    rank = jnp.sum(owner_hot * (jnp.cumsum(owner_hot, axis=0) - 1), axis=1)
    slot = owner * capacity + rank
    slot_ids = (
        jnp.zeros((n_row * capacity,), jnp.int32).at[slot].set(col_local).reshape(n_row, capacity)
    )
    id_rows = jnp.zeros((n_row, 1, feat_q * tile_dim), jnp.bfloat16)
    id_rows = id_rows.at[:, 0, :capacity].set(slot_ids.astype(jnp.bfloat16))
    own_blocks = jnp.take(xb, row_local, axis=0)
    mirror_terms = jnp.einsum(
        "tfi,tij->tfj", own_blocks, tiles, preferred_element_type=jnp.float32
    ).astype(jnp.bfloat16)
    outgoing = jnp.zeros((n_row * capacity, feat_q * tile_dim), jnp.bfloat16)
    outgoing = (
        outgoing.at[slot]
        .set(mirror_terms.reshape(n_tiles, feat_q * tile_dim))
        .reshape(n_row, capacity, feat_q * tile_dim)
    )
    every_block = jnp.broadcast_to(flat_blocks[None], (n_row, n_blocks, feat_q * tile_dim))
    payload = jnp.concatenate([every_block, outgoing, id_rows], axis=1)
    got = lax.all_to_all(payload, "row", split_axis=0, concat_axis=0, tiled=True)
    all_x = got[:, :n_blocks].reshape(n_row * n_blocks, feat_q, tile_dim)
    incoming = got[:, n_blocks : n_blocks + capacity]
    block_ids = got[:, n_blocks + capacity, :capacity].astype(jnp.int32)
    fetched_tiles = jnp.take(all_x, owner * n_blocks + col_local, axis=0)
    forward_terms = jnp.einsum(
        "tfj,tij->tfi", fetched_tiles, tiles, preferred_element_type=jnp.float32
    )
    block_range = jnp.arange(n_blocks, dtype=jnp.int32)
    row_hot = (row_local[:, None] == block_range[None, :]).astype(jnp.float32)
    local_sum = jnp.einsum("tfi,tb->fbi", forward_terms, row_hot, precision=lax.Precision.HIGHEST)
    in_hot = (block_ids.reshape(-1)[:, None] == block_range[None, :]).astype(jnp.bfloat16)
    mirror_sum = jnp.einsum(
        "sk,sb->bk",
        incoming.reshape(n_row * capacity, feat_q * tile_dim),
        in_hot,
        preferred_element_type=jnp.float32,
    )
    mirror_sum = mirror_sum.reshape(n_blocks, feat_q, tile_dim).transpose(1, 0, 2)
    z_part = (local_sum + mirror_sum).reshape(feat_q, rows).astype(jnp.bfloat16)
    z_full = gather_groups(z_part, n_col)
    y_full = lax.dot_general(
        z_full, weight, (((0,), (0,)), ((), ())), preferred_element_type=jnp.float32
    )
    act = jax.nn.silu(y_full).astype(jnp.bfloat16)
    sig = jax.nn.sigmoid(y_full)
    grad_y = (cotangent.astype(jnp.float32) * sig * (1.0 + y_full * (1.0 - sig))).astype(
        jnp.bfloat16
    )
    grad_part = jnp.dot(z_part, grad_y, preferred_element_type=jnp.float32)
    grad_w = sum_over_row(grad_part, n_row)
    return (act, grad_w)


def solution(mesh):
    in_specs = (
        P("col", "row"),
        P("row", None, None),
        P("row", None),
        P("row", None),
        P(),
        P("row", None),
    )
    out_specs = (P("row", None), P("col", None))
    return jax.shard_map(body, mesh=mesh, in_specs=in_specs, out_specs=out_specs, check_vma=False)
```

profile of v0, /device:TPU:0, one launch (start us, length us, event | category | flops | bytes accessed | tf_op | source)
XLA Modules:
  0.0 63.9 jit_solution(13298071320299670246)
XLA Ops:
  0.6 0.8 %fusion.21 = s32[8,8]{1,0:T(8,128)S(1)} fusion(s32[8]{0:T(128)} %bitcast.82), kind=kLoop, calls=%fused_computation.46 | loop fusion | flops 128 | bytes 288 | tf_op jit(solution)/shard_map/convert_element_type | solution.py:44
  1.4 0.8 %select_reduce_fusion = s32[8]{0:T(128)S(1)} fusion(s32[8,8]{1,0:T(8,128)S(1)} %reduce_window_sum.11, s32[8]{0:T(128)} %bitcast.83), kind=kLoop, calls=%fused_computation.44 | loop fusion | flops 248 | bytes 320 | tf_op jit(solution)/shard_map/reduce_sum | solution.py:45
  2.3 0.8 %and_bitcast_fusion.1 = (pred[8]{0:T(512)(128)(4,1)S(1)}, s32[8,1]{0,1:T(1,128)S(1)}, pred[8]{0:T(512)(128)(4,1)S(1)}) fusion(s32[8,2]{0,1:T(2,128)} %param.11, s32[8,1]{0,1:T(1,128)} %param.10), kind=kLoop, calls=%fused_computation.63 | loop fusion | flops 112 | bytes 144 | tf_op jit(solution)/shard_map/jit(_take)/reduce_and | solution.py:68
  3.0 0.8 %slice_bitcast_fusion.2 = (s32[8]{0:T(128)S(1)}, s32[8]{0:T(128)S(1)}, s32[8]{0:T(128)S(1)}, s32[8]{0:T(128)S(1)}) fusion(s32[8,2]{0,1:T(2,128)} %param.11, s32[8]{0:T(128)S(1)} %select_reduce_fusion, s32[8,1]{0,1:T(1,128)} %param.10), kind=kLoop, calls=%fused_computation.72 | loop fusion | flops 64 | bytes 256 | tf_op jit(solution)/shard_map/eq | solution.py:73
  3.8 0.9 %bitcast_bitcast_fusion = (bf16[1,8,32,128]{3,2,1,0:T(8,128)(2,1)S(1)}, bf16[8,32,128]{2,1,0:T(8,128)(2,1)S(1)}) fusion(bf16[32,1024]{1,0:T(8,128)(2,1)} %param.8), kind=kLoop, calls=%fused_computation.28 | loop fusion | bytes 196608
  4.7 0.6 gather_fusion
  5.5 0.8 %scatter_custom_fusion = bf16[16,4096]{1,0:T(8,128)(2,1)S(1)} fusion(s32[8]{0:T(128)S(1)} %get-tuple-element.24, bf16[1,8,32,128]{3,2,1,0:T(8,128)(2,1)S(1)} %fusion.2, bf16[]{:T(256)} %constant.105.clone.1), kind=kCustom, calls=%fused_computation.24 | custom fusion | bytes 196610 | tf_op jit(solution)/shard_map/scatter | solution.py:59
  6.4 0.6 scatter_custom_fusion.1
  7.2 1.1 %fusion.3 = bf16[8,11,4096]{2,1,0:T(8,128)(2,1)} fusion(bf16[8,1,2]{2,1,0:T(2,128)(2,1)S(1)} %convert_element_type.72, bf16[8,2,4096]{2,1,0:T(2,128)(2,1)S(1)} %reshape.155, bf16[8,8,4096]{2,1,0:T(8,128)(2,1)S(1)} %broadcast_in_dim.53), kind=kLoop, calls=%fused_computation.11 | loop fusion | flops 2883584 | bytes 1376288 | tf_op jit(solution)/shard_map/concatenate | solution.py:63
  8.3 7.3 %all-to-all-start = ((bf16[8,11,4096]{2,1,0:T(8,128)(2,1)}), bf16[8,11,4096]{2,1,0:T(8,128)(2,1)S(1)}, u32[]{:S(2)}, u32[]{:S(2)}) async-start(bf16[8,11,4096]{2,1,0:T(8,128)(2,1)} %fusion.3), calls=%async_computation | async-start | bytes 2097152 | tf_op jit(solution)/shard_map/all_to_all | solution.py:64
  15.7 25.6 %all-to-all-done = bf16[8,11,4096]{2,1,0:T(8,128)(2,1)S(1)} async-done(((bf16[8,11,4096]{2,1,0:T(8,128)(2,1)}), bf16[8,11,4096]{2,1,0:T(8,128)(2,1)S(1)}, u32[]{:S(2)}, u32[]{:S(2)}) %all-to-all-start) | async-done | bytes 720928 | tf_op jit(solution)/shard_map/all_to_all | solution.py:64
  41.7 0.6 gather_fusion.1
  43.1 1.6 %collective-permute-start.1 = (bf16[32,1024]{1,0:T(8,128)(2,1)S(1)}, bf16[32,1024]{1,0:T(8,128)(2,1)S(1)}, u32[]{:S(2)}, u32[]{:S(2)}) collective-permute-start(bf16[32,1024]{1,0:T(8,128)(2,1)S(1)} %bitcast.77), channel_id=1, source_target_pairs={{0,2},{1,3},{2,0},{3,1},{4,6},{5,7},{6,4},{7,5},{8,10},{9,11},{10,... | collective-permute-start | bytes 196616 | tf_op jit(solution)/shard_map/ppermute | solution.py:14
  44.6 1.4 %collective-permute-start.2 = (bf16[32,1024]{1,0:T(8,128)(2,1)S(1)}, bf16[32,1024]{1,0:T(8,128)(2,1)S(1)}, u32[]{:S(2)}, u32[]{:S(2)}) collective-permute-start(bf16[32,1024]{1,0:T(8,128)(2,1)S(1)} %bitcast.78), channel_id=1, source_target_pairs={{0,3},{1,0},{2,1},{3,2},{4,7},{5,4},{6,5},{7,6},{8,11},{9,8},{10,9... | collective-permute-start | bytes 196616 | tf_op jit(solution)/shard_map/ppermute | solution.py:14
  46.0 0.8 %collective-permute-done = bf16[32,1024]{1,0:T(8,128)(2,1)S(1)} collective-permute-done((bf16[32,1024]{1,0:T(8,128)(2,1)S(1)}, bf16[32,1024]{1,0:T(8,128)(2,1)S(1)}, u32[]{:S(2)}, u32[]{:S(2)}) %collective-permute-start) | collective-permute-done | bytes 65568 | tf_op jit(solution)/shard_map/ppermute | solution.py:14
  46.8 0.9 %collective-permute-done.1 = bf16[32,1024]{1,0:T(8,128)(2,1)S(1)} collective-permute-done((bf16[32,1024]{1,0:T(8,128)(2,1)S(1)}, bf16[32,1024]{1,0:T(8,128)(2,1)S(1)}, u32[]{:S(2)}, u32[]{:S(2)}) %collective-permute-start.1) | collective-permute-done | bytes 65568 | tf_op jit(solution)/shard_map/ppermute | solution.py:14
  47.9 0.6 gather_fusion.2
  48.6 1.3 %multiply_convert_fusion.1 = (bf16[1024,256]{1,0:T(8,128)(2,1)}, f32[1024,256]{1,0:T(8,128)S(1)}) fusion(bf16[128,1024]{1,0:T(8,128)(2,1)S(1)} %bitcast_select_fusion, bf16[128,256]{1,0:T(8,128)(2,1)S(1)} %copy-done.2), kind=kOutput, calls=%fused_computation.13 | convolution fusion | flops 68419584 | bytes 1900544 | tf_op jit(solution)/shard_map/dot_general | solution.py:85
  49.9 0.5 fusion.4
  50.4 1.5 %collective-permute-start.3 = (f32[32,256]{1,0:T(8,128)S(1)}, f32[32,256]{1,0:T(8,128)S(1)}, u32[]{:S(2)}, u32[]{:S(2)}) collective-permute-start(f32[32,256]{1,0:T(8,128)S(1)} %fusion.4), channel_id=1, source_target_pairs={{0,4},{4,0},{8,12},{12,8},{16,20},{20,16},{24,28},{28,24},{1,5},{5... | collective-permute-start | bytes 98312 | tf_op jit(solution)/shard_map/ppermute | solution.py:27
  51.9 2.6 %collective-permute-done.3 = f32[32,256]{1,0:T(8,128)S(1)} collective-permute-done((f32[32,256]{1,0:T(8,128)S(1)}, f32[32,256]{1,0:T(8,128)S(1)}, u32[]{:S(2)}, u32[]{:S(2)}) %collective-permute-start.3) | collective-permute-done | bytes 32800 | tf_op jit(solution)/shard_map/ppermute | solution.py:27
  54.6 3.9 %collective-permute-done.4 = f32[32,256]{1,0:T(8,128)S(1)} collective-permute-done((f32[32,256]{1,0:T(8,128)S(1)}, f32[32,256]{1,0:T(8,128)S(1)}, u32[]{:S(2)}, u32[]{:S(2)}) %collective-permute-start.4) | collective-permute-done | bytes 32800 | tf_op jit(solution)/shard_map/ppermute | solution.py:27
  58.5 4.8 %collective-permute-done.5 = f32[32,256]{1,0:T(8,128)S(1)} collective-permute-done((f32[32,256]{1,0:T(8,128)S(1)}, f32[32,256]{1,0:T(8,128)S(1)}, u32[]{:S(2)}, u32[]{:S(2)}) %collective-permute-start.5) | collective-permute-done | bytes 32800 | tf_op jit(solution)/shard_map/ppermute | solution.py:27
  63.3 0.6 add.98
  (39 shorter events, 2.2 us)
Async XLA Ops:
  0.6 4.6 %copy-start = (bf16[8,128,128]{2,1,0:T(8,128)(2,1)S(1)}, bf16[8,128,128]{2,1,0:T(8,128)(2,1)}, u32[]{:S(2)}) copy-start(bf16[8,128,128]{2,1,0:T(8,128)(2,1)} %param.9) | copy-start | bytes 786436
  8.3 33.0 %all-to-all-start = ((bf16[8,11,4096]{2,1,0:T(8,128)(2,1)}), bf16[8,11,4096]{2,1,0:T(8,128)(2,1)S(1)}, u32[]{:S(2)}, u32[]{:S(2)}) async-start(bf16[8,11,4096]{2,1,0:T(8,128)(2,1)} %fusion.3), calls=%async_computation | async-start | bytes 2097152 | tf_op jit(solution)/shard_map/all_to_all | solution.py:64
  42.8 5.8 %copy-start.2 = (bf16[128,256]{1,0:T(8,128)(2,1)S(1)}, bf16[128,256]{1,0:T(8,128)(2,1)}, u32[]{:S(2)}) copy-start(bf16[128,256]{1,0:T(8,128)(2,1)} %param.12) | copy-start | bytes 196612
  43.0 3.8 %collective-permute-start = (bf16[32,1024]{1,0:T(8,128)(2,1)S(1)}, bf16[32,1024]{1,0:T(8,128)(2,1)S(1)}, u32[]{:S(2)}, u32[]{:S(2)}) collective-permute-start(bf16[32,1024]{1,0:T(8,128)(2,1)S(1)} %bitcast.76), channel_id=1, source_target_pairs={{0,1},{1,2},{2,3},{3,0},{4,5},{5,6},{6,7},{7,4},{8,9},{9,10},{10,1... | collective-permute-start | bytes 196616 | tf_op jit(solution)/shard_map/ppermute | solution.py:14
  43.1 4.6 %collective-permute-start.1 = (bf16[32,1024]{1,0:T(8,128)(2,1)S(1)}, bf16[32,1024]{1,0:T(8,128)(2,1)S(1)}, u32[]{:S(2)}, u32[]{:S(2)}) collective-permute-start(bf16[32,1024]{1,0:T(8,128)(2,1)S(1)} %bitcast.77), channel_id=1, source_target_pairs={{0,2},{1,3},{2,0},{3,1},{4,6},{5,7},{6,4},{7,5},{8,10},{9,11},{10,... | collective-permute-start | bytes 196616 | tf_op jit(solution)/shard_map/ppermute | solution.py:14
  44.6 3.3 %collective-permute-start.2 = (bf16[32,1024]{1,0:T(8,128)(2,1)S(1)}, bf16[32,1024]{1,0:T(8,128)(2,1)S(1)}, u32[]{:S(2)}, u32[]{:S(2)}) collective-permute-start(bf16[32,1024]{1,0:T(8,128)(2,1)S(1)} %bitcast.78), channel_id=1, source_target_pairs={{0,3},{1,0},{2,1},{3,2},{4,7},{5,4},{6,5},{7,6},{8,11},{9,8},{10,9... | collective-permute-start | bytes 196616 | tf_op jit(solution)/shard_map/ppermute | solution.py:14
  48.6 1.3 %copy-start.1 = (bf16[1024,256]{1,0:T(8,128)(2,1)S(1)}, bf16[1024,256]{1,0:T(8,128)(2,1)}, u32[]{:S(2)}) copy-start(bf16[1024,256]{1,0:T(8,128)(2,1)} %param.13) | copy-start | bytes 1572868
  50.4 4.1 %collective-permute-start.3 = (f32[32,256]{1,0:T(8,128)S(1)}, f32[32,256]{1,0:T(8,128)S(1)}, u32[]{:S(2)}, u32[]{:S(2)}) collective-permute-start(f32[32,256]{1,0:T(8,128)S(1)} %fusion.4), channel_id=1, source_target_pairs={{0,4},{4,0},{8,12},{12,8},{16,20},{20,16},{24,28},{28,24},{1,5},{5... | collective-permute-start | bytes 98312 | tf_op jit(solution)/shard_map/ppermute | solution.py:27
  54.6 3.9 %collective-permute-start.4 = (f32[32,256]{1,0:T(8,128)S(1)}, f32[32,256]{1,0:T(8,128)S(1)}, u32[]{:S(2)}, u32[]{:S(2)}) collective-permute-start(f32[32,256]{1,0:T(8,128)S(1)} %add.96), channel_id=1, source_target_pairs={{0,8},{4,12},{8,0},{12,4},{16,24},{20,28},{24,16},{28,20},{1,9},{5... | collective-permute-start | bytes 98312 | tf_op jit(solution)/shard_map/ppermute | solution.py:27
  58.5 4.8 %collective-permute-start.5 = (f32[32,256]{1,0:T(8,128)S(1)}, f32[32,256]{1,0:T(8,128)S(1)}, u32[]{:S(2)}, u32[]{:S(2)}) collective-permute-start(f32[32,256]{1,0:T(8,128)S(1)} %add.97), channel_id=1, source_target_pairs={{0,16},{4,20},{8,24},{12,28},{16,0},{20,4},{24,8},{28,12},{1,17},{... | collective-permute-start | bytes 98312 | tf_op jit(solution)/shard_map/ppermute | solution.py:27
where the time goes:
time: 64.2 us; the launch traced here: 63.9 us
  waiting for transfers between devices  38.8 us (60%)
  starting transfers between devices  11.8 us (18%)
  other arithmetic  5.09 us (8%)
  local copies, waits for them, and re-layouts  4.72 us (7%)
  matrix products  2.72 us (4%)
  between operations  0.86 us (1%)
    all_to_all x1, waiting for transfers between devices, body(): lax.all_to_all(payload, 'row', split_axis=0, concat_axis=0, tiled=True)  25.6 us
    ppermute x3, waiting for transfers between devices, sum_over_row(): x = x + lax.ppermute(x, 'row', perm)  11.3 us
    all_to_all x1, starting transfers between devices, body(): lax.all_to_all(payload, 'row', split_axis=0, concat_axis=0, tiled=True)  7.28 us
    ppermute x3, starting transfers between devices, gather_groups(): parts.append(lax.ppermute(z_part, 'col', perm))  3 us
    ppermute x3, waiting for transfers between devices, gather_groups(): parts.append(lax.ppermute(z_part, 'col', perm))  1.86 us
    ppermute x3, starting transfers between devices, sum_over_row(): x = x + lax.ppermute(x, 'row', perm)  1.49 us
  transfers between devices with their start and end apart: 7, of which 7 were waited for; matrix products, arithmetic and copies ran while one was open for 0% of the time, Pallas kernels for 0%

commit v1 on v0

--- a/solution.py
+++ b/solution.py
@@ -2,6 +2,33 @@
 import jax.numpy as jnp
 from jax import lax
 from jax.sharding import PartitionSpec as P
+
+
+def build_the_scales(view, array_dim, a0):
+    newest, local_next = (view.shape[:array_dim], view.shape[array_dim + 1 :])
+    current_block = view.reshape(*newest, a0, -1, *local_next)
+    return jnp.moveaxis(current_block, array_dim, 0)
+
+
+def attach_the_circles(values, dimension_no):
+    all_rows = list(values.shape[1:])
+    all_rows[dimension_no] *= values.shape[0]
+    return jnp.moveaxis(values, 0, dimension_no).reshape(all_rows)
+
+
+def advance_racks(v0, shard_in, peer_axis, x_local):
+    now = jax.lax.axis_size(peer_axis)
+    r2 = jax.lax.axis_index(peer_axis)
+    val2, mid_arr = (now, r2)
+    b_next = build_the_scales(v0, shard_in, val2)
+    tray = [b_next[mid_arr]]
+    for no in [*range(1, val2)]:
+        y_new = b_next[mid_arr ^ no]
+        block_last = jax.lax.ppermute(y_new, peer_axis, [(dd, dd ^ no) for dd in range(val2)])
+        tray.append(block_last)
+    plain = jnp.stack(tray, axis=0)
+    b_next = plain[mid_arr ^ jnp.arange(val2)]
+    return attach_the_circles(b_next, x_local)
 
 
 def gather_groups(z_part, n_col):
@@ -61,7 +88,7 @@
     )
     every_block = jnp.broadcast_to(flat_blocks[None], (n_row, n_blocks, feat_q * tile_dim))
     payload = jnp.concatenate([every_block, outgoing, id_rows], axis=1)
-    got = lax.all_to_all(payload, "row", split_axis=0, concat_axis=0, tiled=True)
+    got = advance_racks(payload, 0, "row", 0)
     all_x = got[:, :n_blocks].reshape(n_row * n_blocks, feat_q, tile_dim)
     incoming = got[:, n_blocks : n_blocks + capacity]
     block_ids = got[:, n_blocks + capacity, :capacity].astype(jnp.int32)

time: 64.2 us -> 62.2 us (0.969)
  waiting for transfers between devices: 38.8 us -> 19.6 us
  starting transfers between devices: 11.8 us -> 25.2 us
  local copies, waits for them, and re-layouts: 4.72 us -> 8.22 us
    all_to_all x1 -> x0, waiting for transfers between devices: 25.6 us -> none  [body(): lax.all_to_all(payload, 'row', split_axis=0, concat_axis=0, tiled=True)]
    ppermute x0 -> x7, starting transfers between devices: none -> 12.8 us  [advance_racks(): jax.lax.ppermute(y_new, peer_axis, [(dd, dd ^ no) for dd in range(val2)])]
    ppermute x0 -> x7, waiting for transfers between devices: none -> 10.7 us  [advance_racks(): jax.lax.ppermute(y_new, peer_axis, [(dd, dd ^ no) for dd in range(val2)])]
    ppermute x3, starting transfers between devices: 1.49 us -> 9.32 us  [sum_over_row(): x = x + lax.ppermute(x, 'row', perm)]
    all_to_all x1 -> x0, starting transfers between devices: 7.28 us -> none  [body(): lax.all_to_all(payload, 'row', split_axis=0, concat_axis=0, tiled=True)]
    ppermute x3, waiting for transfers between devices: 11.3 us -> 7.12 us  [sum_over_row(): x = x + lax.ppermute(x, 'row', perm)]
    unnamed x11 -> x22, local copies, waits for them, and re-layouts: 1.05 us -> 3.84 us
    concatenate x1, other arithmetic: 1.1 us -> 0.13 us  [body(): payload = jnp.concatenate([every_block, outgoing, id_rows], axis=1)]
  transfers between devices with their start and end apart: 7 -> 13, of which waited for: 7 -> 7; matrix products, arithmetic and copies ran while one was open for 0% -> 6% of each run, Pallas kernels for 0% -> 0%
where the time goes in v1:
time: 62.2 us; the launch traced here: 61.9 us
  starting transfers between devices  25.2 us (41%)
  waiting for transfers between devices  19.6 us (32%)
  local copies, waits for them, and re-layouts  8.22 us (13%)
  other arithmetic  5.15 us (8%)
  matrix products  2.72 us (4%)
  between operations  1.06 us (2%)
    ppermute x7, starting transfers between devices, advance_racks(): jax.lax.ppermute(y_new, peer_axis, [(dd, dd ^ no) for dd in range(val2)])  12.8 us
    ppermute x7, waiting for transfers between devices, advance_racks(): jax.lax.ppermute(y_new, peer_axis, [(dd, dd ^ no) for dd in range(val2)])  10.7 us
    ppermute x3, starting transfers between devices, sum_over_row(): x = x + lax.ppermute(x, 'row', perm)  9.32 us
    ppermute x3, waiting for transfers between devices, sum_over_row(): x = x + lax.ppermute(x, 'row', perm)  7.12 us
    unnamed x22, local copies, waits for them, and re-layouts  3.84 us
    ppermute x3, starting transfers between devices, gather_groups(): parts.append(lax.ppermute(z_part, 'col', perm))  3 us
    ppermute x3, waiting for transfers between devices, gather_groups(): parts.append(lax.ppermute(z_part, 'col', perm))  1.85 us
    reduce_and x1, other arithmetic, body(): fetched_tiles = jnp.take(all_x, owner * n_blocks + col_local, axis=0)  1.28 us
  transfers between devices with their start and end apart: 13, of which 7 were waited for; matrix products, arithmetic and copies ran while one was open for 6% of the time, Pallas kernels for 0%

profile of v1, /device:TPU:0, one launch (start us, length us, event | category | flops | bytes accessed | tf_op | source)
XLA Modules:
  0.0 61.9 jit_solution(15660003803200795951)
XLA Ops:
  0.7 0.8 %fusion.21 = s32[8,8]{1,0:T(8,128)S(1)} fusion(s32[8]{0:T(128)} %bitcast.114), kind=kLoop, calls=%fused_computation.56 | loop fusion | flops 128 | bytes 288 | tf_op jit(solution)/shard_map/convert_element_type | solution.py:71
  1.5 0.8 %select_reduce_fusion = s32[8]{0:T(128)S(1)} fusion(s32[8,8]{1,0:T(8,128)S(1)} %reduce_window_sum.11, s32[8]{0:T(128)} %bitcast.115), kind=kLoop, calls=%fused_computation.54 | loop fusion | flops 248 | bytes 320 | tf_op jit(solution)/shard_map/reduce_sum | solution.py:72
  2.3 1.3 %and_bitcast_fusion.1 = (pred[8]{0:T(512)(128)(4,1)}, s32[8,1]{0,1:T(1,128)S(1)}, pred[8]{0:T(512)(128)(4,1)S(1)}) fusion(s32[8,2]{0,1:T(2,128)} %param.11, s32[8,1]{0,1:T(1,128)} %param.10), kind=kLoop, calls=%fused_computation.81 | loop fusion | flops 112 | bytes 144 | tf_op jit(solution)/shard_map/jit(_take)/reduce_and | solution.py:95
  4.3 0.9 %bitcast_bitcast_fusion = (bf16[1,8,32,128]{3,2,1,0:T(8,128)(2,1)S(1)}, bf16[8,32,128]{2,1,0:T(8,128)(2,1)S(1)}) fusion(bf16[32,1024]{1,0:T(8,128)(2,1)} %param.8), kind=kLoop, calls=%fused_computation.37 | loop fusion | bytes 196608
  7.9 3.0 %collective-permute-start = (bf16[1,11,4096]{2,1,0:T(8,128)(2,1)S(1)}, bf16[1,11,4096]{2,1,0:T(8,128)(2,1)}, u32[]{:S(2)}, u32[]{:S(2)}) collective-permute-start(bf16[1,11,4096]{2,1,0:T(8,128)(2,1)S(1)} %get-tuple-element.22), channel_id=1, source_target_pairs={{0,4},{4,0},{8,12},{12,8},{16,20},{20,16},{24,28},{28,24},{1,5},{5... | collective-permute-start | bytes 270344 | tf_op jit(solution)/shard_map/ppermute | solution.py:27
  11.0 1.6 %collective-permute-start.1 = (bf16[1,11,4096]{2,1,0:T(8,128)(2,1)S(1)}, bf16[1,11,4096]{2,1,0:T(8,128)(2,1)}, u32[]{:S(2)}, u32[]{:S(2)}) collective-permute-start(bf16[1,11,4096]{2,1,0:T(8,128)(2,1)S(1)} %get-tuple-element.21), channel_id=1, source_target_pairs={{0,8},{4,12},{8,0},{12,4},{16,24},{20,28},{24,16},{28,20},{1,9},{5... | collective-permute-start | bytes 270344 | tf_op jit(solution)/shard_map/ppermute | solution.py:27
  12.6 3.0 %collective-permute-start.3 = (bf16[1,11,4096]{2,1,0:T(8,128)(2,1)S(1)}, bf16[1,11,4096]{2,1,0:T(8,128)(2,1)S(1)}, u32[]{:S(2)}, u32[]{:S(2)}) collective-permute-start(bf16[1,11,4096]{2,1,0:T(8,128)(2,1)S(1)} %get-tuple-element.19), channel_id=1, source_target_pairs={{0,16},{4,20},{8,24},{12,28},{16,0},{20,4},{24,8},{28,12},{1,17},{... | collective-permute-start | bytes 270344 | tf_op jit(solution)/shard_map/ppermute | solution.py:27
  15.5 1.3 %collective-permute-start.4 = (bf16[1,11,4096]{2,1,0:T(8,128)(2,1)S(1)}, bf16[1,11,4096]{2,1,0:T(8,128)(2,1)S(1)}, u32[]{:S(2)}, u32[]{:S(2)}) collective-permute-start(bf16[1,11,4096]{2,1,0:T(8,128)(2,1)S(1)} %get-tuple-element.18), channel_id=1, source_target_pairs={{0,20},{4,16},{8,28},{12,24},{16,4},{20,0},{24,12},{28,8},{1,21},{... | collective-permute-start | bytes 270344 | tf_op jit(solution)/shard_map/ppermute | solution.py:27
  17.6 3.6 %collective-permute-start.5 = (bf16[1,11,4096]{2,1,0:T(8,128)(2,1)S(1)}, bf16[1,11,4096]{2,1,0:T(8,128)(2,1)S(1)}, u32[]{:S(2)}, u32[]{:S(2)}) collective-permute-start(bf16[1,11,4096]{2,1,0:T(8,128)(2,1)S(1)} %get-tuple-element.17), channel_id=1, source_target_pairs={{0,24},{4,28},{8,16},{12,20},{16,8},{20,12},{24,0},{28,4},{1,25},{... | collective-permute-start | bytes 270344 | tf_op jit(solution)/shard_map/ppermute | solution.py:27
  21.2 0.9 %bitcast_dynamic-update-slice_fusion.5 = bf16[8,1,11,4096]{3,2,0,1:T(8,128)(2,1)S(1)} fusion(bf16[8,1,11,4096]{3,2,0,1:T(8,128)(2,1)S(1)} %bitcast_dynamic-update-slice_fusion.7, bf16[1,11,4096]{2,1,0:T(8,128)(2,1)} %collective-permute-done), kind=kLoop, calls=%fused_computation.27 | loop fusion | bytes 221184
  22.5 0.9 %bitcast_dynamic-update-slice_fusion.4 = bf16[8,1,11,4096]{3,2,0,1:T(8,128)(2,1)S(1)} fusion(bf16[8,1,11,4096]{3,2,0,1:T(8,128)(2,1)S(1)} %bitcast_dynamic-update-slice_fusion.5, bf16[1,11,4096]{2,1,0:T(8,128)(2,1)} %collective-permute-done.1), kind=kLoop, calls=%fused_computation.26 | loop fusion | bytes 221184
  23.4 0.9 %bitcast_dynamic-update-slice_fusion.3 = bf16[8,1,11,4096]{3,2,0,1:T(8,128)(2,1)S(1)} fusion(bf16[8,1,11,4096]{3,2,0,1:T(8,128)(2,1)S(1)} %bitcast_dynamic-update-slice_fusion.4, bf16[1,11,4096]{2,1,0:T(8,128)(2,1)} %collective-permute-done.2), kind=kLoop, calls=%fused_computation.25 | loop fusion | bytes 221184
  24.4 10.6 %collective-permute-done.4 = bf16[1,11,4096]{2,1,0:T(8,128)(2,1)S(1)} collective-permute-done((bf16[1,11,4096]{2,1,0:T(8,128)(2,1)S(1)}, bf16[1,11,4096]{2,1,0:T(8,128)(2,1)S(1)}, u32[]{:S(2)}, u32[]{:S(2)}) %collective-permute-start.4) | collective-permute-done | bytes 90144 | tf_op jit(solution)/shard_map/ppermute | solution.py:27
  37.5 1.6 %collective-permute-start.8 = (bf16[32,1024]{1,0:T(8,128)(2,1)S(1)}, bf16[32,1024]{1,0:T(8,128)(2,1)S(1)}, u32[]{:S(2)}, u32[]{:S(2)}) collective-permute-start(bf16[32,1024]{1,0:T(8,128)(2,1)S(1)} %bitcast.109), channel_id=1, source_target_pairs={{0,2},{1,3},{2,0},{3,1},{4,6},{5,7},{6,4},{7,5},{8,10},{9,11},{10,... | collective-permute-start | bytes 196616 | tf_op jit(solution)/shard_map/ppermute | solution.py:41
  39.0 1.4 %collective-permute-start.9 = (bf16[32,1024]{1,0:T(8,128)(2,1)S(1)}, bf16[32,1024]{1,0:T(8,128)(2,1)S(1)}, u32[]{:S(2)}, u32[]{:S(2)}) collective-permute-start(bf16[32,1024]{1,0:T(8,128)(2,1)S(1)} %bitcast.110), channel_id=1, source_target_pairs={{0,3},{1,0},{2,1},{3,2},{4,7},{5,4},{6,5},{7,6},{8,11},{9,8},{10,9... | collective-permute-start | bytes 196616 | tf_op jit(solution)/shard_map/ppermute | solution.py:41
  40.5 0.8 %collective-permute-done.7 = bf16[32,1024]{1,0:T(8,128)(2,1)S(1)} collective-permute-done((bf16[32,1024]{1,0:T(8,128)(2,1)S(1)}, bf16[32,1024]{1,0:T(8,128)(2,1)S(1)}, u32[]{:S(2)}, u32[]{:S(2)}) %collective-permute-start.7) | collective-permute-done | bytes 65568 | tf_op jit(solution)/shard_map/ppermute | solution.py:41
  41.2 0.9 %collective-permute-done.8 = bf16[32,1024]{1,0:T(8,128)(2,1)S(1)} collective-permute-done((bf16[32,1024]{1,0:T(8,128)(2,1)S(1)}, bf16[32,1024]{1,0:T(8,128)(2,1)S(1)}, u32[]{:S(2)}, u32[]{:S(2)}) %collective-permute-start.8) | collective-permute-done | bytes 65568 | tf_op jit(solution)/shard_map/ppermute | solution.py:41
  43.1 1.3 %multiply_convert_fusion.1 = (bf16[1024,256]{1,0:T(8,128)(2,1)}, f32[1024,256]{1,0:T(8,128)S(1)}) fusion(bf16[128,1024]{1,0:T(8,128)(2,1)S(1)} %bitcast_select_fusion, bf16[128,256]{1,0:T(8,128)(2,1)S(1)} %copy-done.4), kind=kOutput, calls=%fused_computation.14 | convolution fusion | flops 68419584 | bytes 1900544 | tf_op jit(solution)/shard_map/dot_general | solution.py:112
  44.9 0.8 %collective-permute-start.10 = (f32[32,256]{1,0:T(8,128)S(1)}, f32[32,256]{1,0:T(8,128)S(1)}, u32[]{:S(2)}, u32[]{:S(2)}) collective-permute-start(f32[32,256]{1,0:T(8,128)S(1)} %fusion.4), channel_id=1, source_target_pairs={{0,4},{4,0},{8,12},{12,8},{16,20},{20,16},{24,28},{28,24},{1,5},{5... | collective-permute-start | bytes 98312 | tf_op jit(solution)/shard_map/ppermute | solution.py:54
  45.6 3.3 %collective-permute-done.10 = f32[32,256]{1,0:T(8,128)S(1)} collective-permute-done((f32[32,256]{1,0:T(8,128)S(1)}, f32[32,256]{1,0:T(8,128)S(1)}, u32[]{:S(2)}, u32[]{:S(2)}) %collective-permute-start.10) | collective-permute-done | bytes 32800 | tf_op jit(solution)/shard_map/ppermute | solution.py:54
  49.0 5.0 %collective-permute-start.11 = (f32[32,256]{1,0:T(8,128)S(1)}, f32[32,256]{1,0:T(8,128)S(1)}, u32[]{:S(2)}, u32[]{:S(2)}) collective-permute-start(f32[32,256]{1,0:T(8,128)S(1)} %add.139), channel_id=1, source_target_pairs={{0,8},{4,12},{8,0},{12,4},{16,24},{20,28},{24,16},{28,20},{1,9},{5... | collective-permute-start | bytes 98312 | tf_op jit(solution)/shard_map/ppermute | solution.py:54
  54.0 1.9 %collective-permute-done.11 = f32[32,256]{1,0:T(8,128)S(1)} collective-permute-done((f32[32,256]{1,0:T(8,128)S(1)}, f32[32,256]{1,0:T(8,128)S(1)}, u32[]{:S(2)}, u32[]{:S(2)}) %collective-permute-start.11) | collective-permute-done | bytes 32800 | tf_op jit(solution)/shard_map/ppermute | solution.py:54
  55.9 3.5 %collective-permute-start.12 = (f32[32,256]{1,0:T(8,128)S(1)}, f32[32,256]{1,0:T(8,128)S(1)}, u32[]{:S(2)}, u32[]{:S(2)}) collective-permute-start(f32[32,256]{1,0:T(8,128)S(1)} %add.140), channel_id=1, source_target_pairs={{0,16},{4,20},{8,24},{12,28},{16,0},{20,4},{24,8},{28,12},{1,17},{... | collective-permute-start | bytes 98312 | tf_op jit(solution)/shard_map/ppermute | solution.py:54
  59.4 1.9 %collective-permute-done.12 = f32[32,256]{1,0:T(8,128)S(1)} collective-permute-done((f32[32,256]{1,0:T(8,128)S(1)}, f32[32,256]{1,0:T(8,128)S(1)}, u32[]{:S(2)}, u32[]{:S(2)}) %collective-permute-start.12) | collective-permute-done | bytes 32800 | tf_op jit(solution)/shard_map/ppermute | solution.py:54
  (67 shorter events, 9.0 us)
Async XLA Ops:
  0.6 5.1 %copy-start = (bf16[8,128,128]{2,1,0:T(8,128)(2,1)S(1)}, bf16[8,128,128]{2,1,0:T(8,128)(2,1)}, u32[]{:S(2)}) copy-start(bf16[8,128,128]{2,1,0:T(8,128)(2,1)} %param.9) | copy-start | bytes 786436
  7.9 9.6 %collective-permute-start = (bf16[1,11,4096]{2,1,0:T(8,128)(2,1)S(1)}, bf16[1,11,4096]{2,1,0:T(8,128)(2,1)}, u32[]{:S(2)}, u32[]{:S(2)}) collective-permute-start(bf16[1,11,4096]{2,1,0:T(8,128)(2,1)S(1)} %get-tuple-element.22), channel_id=1, source_target_pairs={{0,4},{4,0},{8,12},{12,8},{16,20},{20,16},{24,28},{28,24},{1,5},{5... | collective-permute-start | bytes 270344 | tf_op jit(solution)/shard_map/ppermute | solution.py:27
  11.0 11.1 %collective-permute-start.1 = (bf16[1,11,4096]{2,1,0:T(8,128)(2,1)S(1)}, bf16[1,11,4096]{2,1,0:T(8,128)(2,1)}, u32[]{:S(2)}, u32[]{:S(2)}) collective-permute-start(bf16[1,11,4096]{2,1,0:T(8,128)(2,1)S(1)} %get-tuple-element.21), channel_id=1, source_target_pairs={{0,8},{4,12},{8,0},{12,4},{16,24},{20,28},{24,16},{28,20},{1,9},{5... | collective-permute-start | bytes 270344 | tf_op jit(solution)/shard_map/ppermute | solution.py:27
  12.6 10.8 %collective-permute-start.2 = (bf16[1,11,4096]{2,1,0:T(8,128)(2,1)S(1)}, bf16[1,11,4096]{2,1,0:T(8,128)(2,1)}, u32[]{:S(2)}, u32[]{:S(2)}) collective-permute-start(bf16[1,11,4096]{2,1,0:T(8,128)(2,1)S(1)} %get-tuple-element.20), channel_id=1, source_target_pairs={{0,12},{4,8},{8,4},{12,0},{16,28},{20,24},{24,20},{28,16},{1,13},{... | collective-permute-start | bytes 270344 | tf_op jit(solution)/shard_map/ppermute | solution.py:27
  12.6 11.8 %collective-permute-start.3 = (bf16[1,11,4096]{2,1,0:T(8,128)(2,1)S(1)}, bf16[1,11,4096]{2,1,0:T(8,128)(2,1)S(1)}, u32[]{:S(2)}, u32[]{:S(2)}) collective-permute-start(bf16[1,11,4096]{2,1,0:T(8,128)(2,1)S(1)} %get-tuple-element.19), channel_id=1, source_target_pairs={{0,16},{4,20},{8,24},{12,28},{16,0},{20,4},{24,8},{28,12},{1,17},{... | collective-permute-start | bytes 270344 | tf_op jit(solution)/shard_map/ppermute | solution.py:27
  15.5 19.4 %collective-permute-start.4 = (bf16[1,11,4096]{2,1,0:T(8,128)(2,1)S(1)}, bf16[1,11,4096]{2,1,0:T(8,128)(2,1)S(1)}, u32[]{:S(2)}, u32[]{:S(2)}) collective-permute-start(bf16[1,11,4096]{2,1,0:T(8,128)(2,1)S(1)} %get-tuple-element.18), channel_id=1, source_target_pairs={{0,20},{4,16},{8,28},{12,24},{16,4},{20,0},{24,12},{28,8},{1,21},{... | collective-permute-start | bytes 270344 | tf_op jit(solution)/shard_map/ppermute | solution.py:27
  17.6 17.4 %collective-permute-start.5 = (bf16[1,11,4096]{2,1,0:T(8,128)(2,1)S(1)}, bf16[1,11,4096]{2,1,0:T(8,128)(2,1)S(1)}, u32[]{:S(2)}, u32[]{:S(2)}) collective-permute-start(bf16[1,11,4096]{2,1,0:T(8,128)(2,1)S(1)} %get-tuple-element.17), channel_id=1, source_target_pairs={{0,24},{4,28},{8,16},{12,20},{16,8},{20,12},{24,0},{28,4},{1,25},{... | collective-permute-start | bytes 270344 | tf_op jit(solution)/shard_map/ppermute | solution.py:27
  22.1 12.9 %collective-permute-start.6 = (bf16[1,11,4096]{2,1,0:T(8,128)(2,1)S(1)}, bf16[1,11,4096]{2,1,0:T(8,128)(2,1)S(1)}, u32[]{:S(2)}, u32[]{:S(2)}) collective-permute-start(bf16[1,11,4096]{2,1,0:T(8,128)(2,1)S(1)} %get-tuple-element.16), channel_id=1, source_target_pairs={{0,28},{4,24},{8,20},{12,16},{16,12},{20,8},{24,4},{28,0},{1,29},{... | collective-permute-start | bytes 270344 | tf_op jit(solution)/shard_map/ppermute | solution.py:27
  35.7 0.9 %copy-start.1 = (pred[8]{0:T(512)(128)(4,1)S(1)}, pred[8]{0:T(512)(128)(4,1)}, u32[]{:S(2)}) copy-start(pred[8]{0:T(512)(128)(4,1)} %get-tuple-element.14) | copy-start | bytes 28
  35.9 4.5 %copy-start.2 = (s32[4]{0:T(128)S(1)}, s32[4]{0:T(128)}, u32[]{:S(2)}) copy-start(s32[4]{0:T(128)} %fusion.32) | copy-start | bytes 52
  37.2 5.8 %copy-start.4 = (bf16[128,256]{1,0:T(8,128)(2,1)S(1)}, bf16[128,256]{1,0:T(8,128)(2,1)}, u32[]{:S(2)}) copy-start(bf16[128,256]{1,0:T(8,128)(2,1)} %param.12) | copy-start | bytes 196612
  37.4 3.8 %collective-permute-start.7 = (bf16[32,1024]{1,0:T(8,128)(2,1)S(1)}, bf16[32,1024]{1,0:T(8,128)(2,1)S(1)}, u32[]{:S(2)}, u32[]{:S(2)}) collective-permute-start(bf16[32,1024]{1,0:T(8,128)(2,1)S(1)} %bitcast.108), channel_id=1, source_target_pairs={{0,1},{1,2},{2,3},{3,0},{4,5},{5,6},{6,7},{7,4},{8,9},{9,10},{10,1... | collective-permute-start | bytes 196616 | tf_op jit(solution)/shard_map/ppermute | solution.py:41
  37.5 4.6 %collective-permute-start.8 = (bf16[32,1024]{1,0:T(8,128)(2,1)S(1)}, bf16[32,1024]{1,0:T(8,128)(2,1)S(1)}, u32[]{:S(2)}, u32[]{:S(2)}) collective-permute-start(bf16[32,1024]{1,0:T(8,128)(2,1)S(1)} %bitcast.109), channel_id=1, source_target_pairs={{0,2},{1,3},{2,0},{3,1},{4,6},{5,7},{6,4},{7,5},{8,10},{9,11},{10,... | collective-permute-start | bytes 196616 | tf_op jit(solution)/shard_map/ppermute | solution.py:41
  39.0 3.3 %collective-permute-start.9 = (bf16[32,1024]{1,0:T(8,128)(2,1)S(1)}, bf16[32,1024]{1,0:T(8,128)(2,1)S(1)}, u32[]{:S(2)}, u32[]{:S(2)}) collective-permute-start(bf16[32,1024]{1,0:T(8,128)(2,1)S(1)} %bitcast.110), channel_id=1, source_target_pairs={{0,3},{1,0},{2,1},{3,2},{4,7},{5,4},{6,5},{7,6},{8,11},{9,8},{10,9... | collective-permute-start | bytes 196616 | tf_op jit(solution)/shard_map/ppermute | solution.py:41
  43.0 1.3 %copy-start.3 = (bf16[1024,256]{1,0:T(8,128)(2,1)S(1)}, bf16[1024,256]{1,0:T(8,128)(2,1)}, u32[]{:S(2)}) copy-start(bf16[1024,256]{1,0:T(8,128)(2,1)} %param.13) | copy-start | bytes 1572868
  44.9 4.1 %collective-permute-start.10 = (f32[32,256]{1,0:T(8,128)S(1)}, f32[32,256]{1,0:T(8,128)S(1)}, u32[]{:S(2)}, u32[]{:S(2)}) collective-permute-start(f32[32,256]{1,0:T(8,128)S(1)} %fusion.4), channel_id=1, source_target_pairs={{0,4},{4,0},{8,12},{12,8},{16,20},{20,16},{24,28},{28,24},{1,5},{5... | collective-permute-start | bytes 98312 | tf_op jit(solution)/shard_map/ppermute | solution.py:54
  49.0 6.9 %collective-permute-start.11 = (f32[32,256]{1,0:T(8,128)S(1)}, f32[32,256]{1,0:T(8,128)S(1)}, u32[]{:S(2)}, u32[]{:S(2)}) collective-permute-start(f32[32,256]{1,0:T(8,128)S(1)} %add.139), channel_id=1, source_target_pairs={{0,8},{4,12},{8,0},{12,4},{16,24},{20,28},{24,16},{28,20},{1,9},{5... | collective-permute-start | bytes 98312 | tf_op jit(solution)/shard_map/ppermute | solution.py:54
  55.9 5.4 %collective-permute-start.12 = (f32[32,256]{1,0:T(8,128)S(1)}, f32[32,256]{1,0:T(8,128)S(1)}, u32[]{:S(2)}, u32[]{:S(2)}) collective-permute-start(f32[32,256]{1,0:T(8,128)S(1)} %add.140), channel_id=1, source_target_pairs={{0,16},{4,20},{8,24},{12,28},{16,0},{20,4},{24,8},{28,12},{1,17},{... | collective-permute-start | bytes 98312 | tf_op jit(solution)/shard_map/ppermute | solution.py:54
